TPU v7x, 512 devices: a whole 4x8x8 slice. The times are simulated.
512 devices in a mesh: req: 64 (over z, x, core), tp: 8 (over y).
Axes of the slice: x: 4, y: 8, z: 8, core: 2. Of those that a mesh axis runs over, the one named last changes fastest.
Arguments:
- q_new: bfloat16 [4096, 5120], P('req', 'tp'), may hold values from -6 to 6
- k_new: bfloat16 [4096, 1024], P('req', 'tp'), may hold values from -15 to 15
- v_new: bfloat16 [4096, 1024], P('req', 'tp'), may hold values from -6 to 6
- k_cache: bfloat16 [1024, 128, 1024], P('req', None, 'tp'), may hold values from -16 to 16
- v_cache: bfloat16 [1024, 128, 1024], P('req', None, 'tp'), may hold values from -6 to 6
- lengths: int32 [32], replicated, may hold values from 1 to 4096, as said below
- page_table: int32 [32, 32], replicated, may hold values from -1 to 1023, as said below
- w_out: bfloat16 [5120, 5120], P('req', 'tp'), may hold values from -0.078125 to 0.078125
Outputs:
- attn_out: bfloat16 [4096, 5120], P('req')
Inputs may be any that keep to these rules, and one draw needn't show every extreme that they name: `lengths`: the last request, 31, has exactly 4096 cached tokens; every request has at least one. `page_table`: request r uses ceil(lengths[r] / 128) logical pages. Its first ceil(ceil(lengths[r] / 128) / 2) logical pages lie among global pages 2r * 16 to (2r + 1) * 16 - 1, the rest among (2r + 1) * 16 to (2r + 2) * 16 - 1; distinct logical pages use distinct global pages; entries past a request's last page are -1.
All inputs are finite; a program needn't handle non-finite values.
Results may differ from a plain program's by a relative error of at most 0.024.
Values may be sent and summed in bfloat16 or wider, within the bound.
No kernel may reach another device: no remote copies, remote signals or barrier semaphores. Data moves between devices by JAX's collectives and lax.ppermute only.
A program may use at most 64 MiB of HBM per device.

v0:
```python
import math
import jax
import jax.numpy as jnp
from jax import lax
from jax.sharding import Mesh
from jax.sharding import PartitionSpec as P

HD = 128
GROUP = 5
ROWS = ("z", "x", "core")
ROPE_BASE = 1000000.0
FLOOR_SCORE = -1e30


def from_partner(value, axis, distance):
    return lax.ppermute(value, axis, [(i, i ^ 1 << distance) for i in range(lax.axis_size(axis))])


def rotate(values, places):
    inverse = 1.0 / ROPE_BASE ** (jnp.arange(0, HD, 2).astype(jnp.float32) / HD)
    angles = places.astype(jnp.float32)[:, None] * inverse[None, :]
    cosine = jnp.concatenate([jnp.cos(angles), jnp.cos(angles)], axis=-1)[:, None, :]
    sine = jnp.concatenate([jnp.sin(angles), jnp.sin(angles)], axis=-1)[:, None, :]
    first_half = values[..., : HD // 2]
    second_half = values[..., HD // 2 :]
    turned = jnp.concatenate([-second_half, first_half], axis=-1)
    return values * cosine + turned * sine


def absorb(state, queries, block_keys, block_values, allowed, scale):
    running_max, running_sum, output = state
    scores = (
        jnp.einsum("qcgd,kcd->cgqk", queries, block_keys, preferred_element_type=jnp.float32)
        * scale
    )
    scores = jnp.where(allowed[None, None], scores, FLOOR_SCORE)
    new_max = jnp.maximum(running_max, jnp.max(scores, axis=-1))
    factor = jnp.exp(running_max - new_max)
    weights = jnp.where(allowed[None, None], jnp.exp(scores - new_max[..., None]), 0.0)
    running_sum = running_sum * factor + jnp.sum(weights, axis=-1)
    mixed = jnp.einsum(
        "cgqk,kcd->qcgd",
        weights.astype(jnp.bfloat16),
        block_values,
        preferred_element_type=jnp.float32,
    )
    output = output * jnp.transpose(factor, (2, 0, 1))[..., None] + mixed
    return (new_max, running_sum, output)


def output_rows(w_out):
    parts = lax.axis_size("tp")
    rows, width = w_out.shape
    share = rows // parts
    pieces = lax.all_to_all(w_out.reshape(parts, share, width), "tp", 0, 0, tiled=True)
    mine = jnp.transpose(pieces, (1, 0, 2))
    near = lax.all_gather(mine, "z", axis=0, tiled=True)
    return (lax.all_gather(near, ("x", "core"), axis=0, tiled=True), share)


def shards(q_new, k_new, v_new, k_cache, v_cache, lengths, page_table, w_out):
    own_rows = q_new.shape[0]
    all_rows = 2 * own_rows
    local_heads = k_new.shape[1] // HD
    pages_local = k_cache.shape[0]
    page_rows = k_cache.shape[1]
    scale = 1.0 / math.sqrt(HD)
    weights_mine, share = output_rows(w_out)
    device_row = (lax.axis_index("z") * lax.axis_size("x") + lax.axis_index("x")) * lax.axis_size(
        "core"
    ) + lax.axis_index("core")
    parity = device_row % 2
    request = device_row // 2
    length = lengths[request]
    own_places = length + parity * own_rows + jnp.arange(own_rows)
    own_queries = rotate(
        q_new.reshape(own_rows, local_heads * GROUP, HD).astype(jnp.float32), own_places
    ).astype(jnp.bfloat16)
    own_keys = rotate(
        k_new.reshape(own_rows, local_heads, HD).astype(jnp.float32), own_places
    ).astype(jnp.bfloat16)
    own_values = v_new.reshape(own_rows, local_heads, HD)
    query_heads = own_queries.shape[1]
    peer_pack = from_partner(
        jnp.concatenate([own_queries, own_keys, own_values], axis=1), "core", 0
    )
    peer_queries = peer_pack[:, :query_heads]
    peer_keys = peer_pack[:, query_heads : query_heads + local_heads]
    peer_values = peer_pack[:, query_heads + local_heads :]

    def ordered(mine, theirs):
        return jnp.where(
            parity == 0,
            jnp.concatenate([mine, theirs], axis=0),
            jnp.concatenate([theirs, mine], axis=0),
        )

    queries = ordered(own_queries, peer_queries).reshape(all_rows, local_heads, GROUP, HD)
    fresh_keys = ordered(own_keys, peer_keys)
    fresh_values = ordered(own_values, peer_values)
    state = (
        jnp.full((local_heads, GROUP, all_rows), FLOOR_SCORE, jnp.float32),
        jnp.zeros((local_heads, GROUP, all_rows), jnp.float32),
        jnp.zeros((all_rows, local_heads, GROUP, HD), jnp.float32),
    )
    token_index = jnp.arange(all_rows)
    causal = (token_index[None, :] <= token_index[:, None]) & (parity == 1)
    state = absorb(state, queries, fresh_keys, fresh_values, causal, scale)
    page_count = (length + page_rows - 1) // page_rows
    even_pages = (page_count + 1) // 2
    first_page = jnp.where(parity == 0, 0, even_pages)
    last_page = jnp.where(parity == 0, even_pages, page_count)
    table_row = page_table[request]
    logical = jnp.arange(table_row.shape[0])
    in_range = (logical >= first_page) & (logical < last_page)
    offset = device_row * pages_local
    slot_ids = jnp.arange(pages_local)
    match = in_range[:, None] & (table_row[:, None] - offset == slot_ids[None, :])
    used = jnp.any(match, axis=0)
    base = jnp.sum(jnp.where(match, logical[:, None], 0), axis=0) * page_rows
    key_places = (base[:, None] + jnp.arange(page_rows)[None, :]).reshape(-1)
    usable = jnp.repeat(used, page_rows) & (key_places < length)
    allowed = jnp.broadcast_to(usable[None, :], (all_rows, pages_local * page_rows))
    pool_keys = k_cache.reshape(pages_local * page_rows, local_heads, HD)
    pool_values = v_cache.reshape(pages_local * page_rows, local_heads, HD)
    half = pool_keys.shape[0] // 2
    for start in (0, half):
        state = absorb(
            state,
            queries,
            pool_keys[start : start + half],
            pool_values[start : start + half],
            allowed[:, start : start + half],
            scale,
        )
    running_max, running_sum, output = state
    peer_start = (1 - parity) * own_rows
    own_start = parity * own_rows
    outgoing = (
        lax.dynamic_slice_in_dim(output, peer_start, own_rows, 0),
        lax.dynamic_slice_in_dim(running_max, peer_start, own_rows, 2),
        lax.dynamic_slice_in_dim(running_sum, peer_start, own_rows, 2),
    )
    outgoing = jnp.concatenate(
        [
            outgoing[0].astype(jnp.bfloat16),
            jnp.transpose(outgoing[1], (2, 0, 1))[..., None].astype(jnp.bfloat16),
            jnp.transpose(outgoing[2], (2, 0, 1))[..., None].astype(jnp.bfloat16),
        ],
        axis=-1,
    )
    incoming = from_partner(outgoing, "core", 0).astype(jnp.float32)
    other_output = incoming[..., :HD]
    other_max = jnp.transpose(incoming[..., HD], (1, 2, 0))
    other_sum = jnp.transpose(incoming[..., HD + 1], (1, 2, 0))
    mine_output = lax.dynamic_slice_in_dim(output, own_start, own_rows, 0)
    mine_max = lax.dynamic_slice_in_dim(running_max, own_start, own_rows, 2)
    mine_sum = lax.dynamic_slice_in_dim(running_sum, own_start, own_rows, 2)
    joint_max = jnp.maximum(mine_max, other_max)
    mine_factor = jnp.exp(mine_max - joint_max)
    other_factor = jnp.exp(other_max - joint_max)
    joint_sum = mine_sum * mine_factor + other_sum * other_factor
    joint_output = (
        mine_output * jnp.transpose(mine_factor, (2, 0, 1))[..., None]
        + other_output * jnp.transpose(other_factor, (2, 0, 1))[..., None]
    )
    attention = (
        (joint_output / jnp.transpose(joint_sum, (2, 0, 1))[..., None])
        .reshape(own_rows, local_heads * GROUP * HD)
        .astype(jnp.bfloat16)
    )
    full_rows = lax.all_gather(attention[:, None], "tp", axis=1, tiled=True)
    projected = lax.dot_general(
        full_rows, weights_mine, (((1, 2), (1, 2)), ((), ())), preferred_element_type=jnp.float32
    )
    depth = lax.axis_size("z")
    projected = projected.reshape(own_rows, -1, depth, share)
    projected = jnp.transpose(projected, (0, 2, 1, 3)).reshape(own_rows, -1, share)
    projected = projected.astype(jnp.bfloat16)
    gathered = lax.all_gather(projected, "tp", axis=2, tiled=True)
    return gathered.reshape(own_rows, -1)


def solution(mesh):
    in_specs = (
        P(ROWS, "tp"),
        P(ROWS, "tp"),
        P(ROWS, "tp"),
        P(ROWS, None, "tp"),
        P(ROWS, None, "tp"),
        P(),
        P(),
        P(ROWS, "tp"),
    )
    out_specs = P(ROWS, None)
    rows, parts = mesh.devices.shape
    cores = 2
    depth = 4 if rows % (4 * cores) == 0 else 1
    split = Mesh(mesh.devices.reshape(depth, rows // (depth * cores), cores, parts), ROWS + ("tp",))
    return jax.shard_map(
        shards, mesh=split, in_specs=in_specs, out_specs=out_specs, check_vma=False
    )
```

profile of v0, /device:TPU:6, one launch (start us, length us, event | category | flops | bytes accessed | tf_op | source)
XLA Modules:
  0.0 135.1 jit_solution(9151260461402743674)
XLA Ops:
  6.5 0.0 all-gather.2.cloned.1.call-start
  6.6 1.0 reshape.452
  7.6 16.7 %all_to_all.5 = bf16[8,10,640]{2,1,0:T(8,128)(2,1)S(1)} all-to-all(bf16[8,10,640]{2,1,0:T(8,128)(2,1)S(1)} %reshape.452), channel_id=1, replica_groups=mesh['z'=4,'x'=8,'core'=2,'tp'=8] {'tp'}, dimensions={0} | all-to-all | bytes 204800 | tf_op jit(solution)/shard_map/all_to_all | solution.py:55
  24.3 21.0 %all_gather.13 = bf16[40,8,640]{2,1,0:T(8,128)(2,1)S(1)} all-gather(bf16[10,8,640]{2,1,0:T(8,128)(2,1)S(1)} %copy.92), channel_id=1, replica_groups=mesh['z'=4,'x'=8,'core'=2,'tp'=8] {'z'}, dimensions={0}, use_global_device_ids=true | all-gather | bytes 512000 | tf_op jit(solution)/shard_map/all_gather | solution.py:57
  45.3 0.8 copy.93
  46.1 0.1 reshape.454
  46.2 0.6 dynamic_slice.24
  47.5 0.2 multiply_cosine_fusion
  47.7 0.1 fusion.54
  47.8 0.1 pad_maximum_fusion.2
  48.0 0.1 slice_negate_fusion
  48.1 0.1 fusion.41
  48.3 0.1 pad_maximum_fusion.1
  48.4 1.9 %collective-permute-start = (bf16[64,7,128]{2,1,0:T(8,128)(2,1)S(1)}, bf16[64,7,128]{2,1,0:T(8,128)(2,1)S(1)}, u32[]{:S(2)}, u32[]{:S(2)}) collective-permute-start(bf16[64,7,128]{2,1,0:T(8,128)(2,1)S(1)} %pad_maximum_fusion.1), channel_id=1, source_target_pairs={{0,8},{8,0},{1,9},{9,1},{2,10},{10,2},{3,11},{11,3},{4,12},{12,4},... | collective-permute-start | bytes 344072 | tf_op jit(solution)/shard_map/ppermute | solution.py:16
  51.1 0.7 fusion.97
  51.8 0.1 fusion.77
  51.9 0.1 select_reduce_fusion
  52.0 0.7 fusion.79
  52.8 0.8 fusion.110
  53.6 0.1 fusion.112
  53.7 0.1 maximum_select_fusion
  53.9 0.2 fusion.113
  54.1 0.6 fusion.2
  54.7 0.6 fusion.3
  55.4 0.1 fusion.38
  55.4 1.5 %fusion.4 = (f32[5,128]{1,0:T(8,128)S(1)}, f32[5,128]{1,0:T(8,128)S(1)}) fusion(f32[128,5,1024]{2,0,1:T(8,128)S(1)} %get-tuple-element.38, f32[5,128]{1,0:T(8,128)S(1)} %get-tuple-element.10, pred[1024]{0:T(1024)(128)(4,1)S(1)} %get-tuple-element.8, f32[5,128]{1,0:T(8,128)S(1)} %get-tuple-element.9, f32[128,5,1024]{2,0,1:T(8,128)S(1)} %get-tuple-element.36, ...), kind=kLoop, calls=%fused_computation.8 | loop fusion | flops 6552320 | bytes 5255168 | tf_op jit(solution)/shard_map/reduce_sum | solution.py:40
  57.0 0.1 fusion.90
  57.0 0.1 copy.87
  57.2 0.1 fusion.91
  57.3 0.1 copy.88
  57.4 0.3 fusion.35
  57.7 2.5 %fusion.31 = f32[128,1,5,128]{3,0,2,1:T(8,128)S(1)} fusion(f32[128,1,5,128]{3,0,2,1:T(8,128)S(1)} %fusion.35, bf16[1024,128,1]{1,0,2:T(8,128)(2,1)} %bitcast.311, f32[128,5,1024]{2,0,1:T(8,128)} %copy-done, f32[5,128]{1,0:T(8,128)S(1)} %get-tuple-element.10, pred[1024]{0:T(1024)(128)(4,1)S(1)} %get-tuple-element.8, f32[128,5]{0,1:T(8,128)S(1)} %get-tuple-element.24), kind=kOutput, calls=%fused_computation.27 | convolution fusion | flops 171212800 | bytes 3545088 | tf_op jit(solution)/shard_map/cgqk,kcd->qcgd/dot_general | solution.py:41
  60.2 0.7 fusion.28
  61.0 0.1 pad_maximum_fusion
  61.1 2.4 %collective-permute-start.1 = (bf16[64,1,5,130]{3,0,2,1:T(8,128)(2,1)S(1)}, bf16[64,1,5,130]{3,0,2,1:T(8,128)(2,1)S(1)}, u32[]{:S(2)}, u32[]{:S(2)}) collective-permute-start(bf16[64,1,5,130]{3,0,2,1:T(8,128)(2,1)S(1)} %pad_maximum_fusion), channel_id=1, source_target_pairs={{0,8},{8,0},{1,9},{9,1},{2,10},{10,2},{3,11},{11,3},{4,12},{12,4},... | collective-permute-start | bytes 249608 | tf_op jit(solution)/shard_map/ppermute | solution.py:16
  63.5 1.0 collective-permute-done.1
  64.5 0.2 slice_reduce_fusion.1
  64.8 0.1 fusion.95
  64.8 0.2 copy_bitcast_fusion
  65.1 25.7 %all_gather.12 = bf16[64,8,640]{2,0,1:T(8,128)(2,1)S(1)} all-gather(bf16[64,1,640]{2,0,1:T(8,128)(2,1)S(1)} %copy_bitcast_fusion), channel_id=1, replica_groups=mesh['z'=4,'x'=8,'core'=2,'tp'=8] {'tp'}, dimensions={1}, use_global_device_ids=true | all-gather | bytes 737280 | tf_op jit(solution)/shard_map/all_gather | solution.py:172
  90.7 4.9 %fusion.37 = bf16[64,640]{1,0:T(8,128)(2,1)S(1)} fusion(bf16[64,8,640]{2,0,1:T(8,128)(2,1)S(1)} %all_gather.12, bf16[640,8,640]{2,0,1:T(8,128)(2,1)} %all-gather.2.cloned.1.call-done), kind=kOutput, calls=%fused_computation.32 | convolution fusion | flops 419471360 | bytes 7290880 | tf_op jit(solution)/shard_map/dot_general | solution.py:173
  95.7 0.2 copy.94
  95.8 0.1 convert_element_type.134
  95.9 0.1 copy.95
  96.0 0.1 copy.96
  96.2 27.6 %all_gather.15 = bf16[64,64,80]{1,0,2:T(8,128)(2,1)S(1)} all-gather(bf16[64,64,10]{1,0,2:T(8,128)(2,1)S(1)} %copy.96), channel_id=1, replica_groups=mesh['z'=4,'x'=8,'core'=2,'tp'=8] {'tp'}, dimensions={2}, use_global_device_ids=true | all-gather | bytes 737280 | tf_op jit(solution)/shard_map/all_gather | solution.py:180
  123.8 1.5 %copy.97 = bf16[64,64,80]{2,1,0:T(8,128)(2,1)S(1)} copy(bf16[64,64,80]{1,0,2:T(8,128)(2,1)S(1)} %all_gather.15) | data formatting | bytes 1310720 | tf_op jit(solution)/shard_map/all_gather | solution.py:180
  125.3 2.9 %reshape.453 = bf16[64,5120]{1,0:T(8,128)(2,1)} reshape(bf16[64,64,80]{2,1,0:T(8,128)(2,1)S(1)} %copy.97) | data formatting | bytes 1310720 | tf_op jit(solution)/shard_map/reshape | solution.py:181
  (35 shorter events, 0.3 us)
Async XLA Ops:
  6.5 39.6 %copy-start.3 = (bf16[64,640]{1,0:T(8,128)(2,1)S(1)}, bf16[64,640]{1,0:T(8,128)(2,1)}, u32[]{:S(2)}) copy-start(bf16[64,640]{1,0:T(8,128)(2,1)} %param.8) | copy-start | bytes 245764
  6.5 39.7 %copy-start.6 = (s32[32]{0:T(128)S(1)}, s32[32]{0:T(128)}, u32[]{:S(2)}) copy-start(s32[32]{0:T(128)} %param.13) | copy-start | bytes 388
  6.5 41.0 %copy-start.4 = (bf16[64,128]{1,0:T(8,128)(2,1)S(1)}, bf16[64,128]{1,0:T(8,128)(2,1)}, u32[]{:S(2)}) copy-start(bf16[64,128]{1,0:T(8,128)(2,1)} %param.9) | copy-start | bytes 49156
  6.5 41.4 %copy-start.5 = (bf16[64,128]{1,0:T(8,128)(2,1)S(1)}, bf16[64,128]{1,0:T(8,128)(2,1)}, u32[]{:S(2)}) copy-start(bf16[64,128]{1,0:T(8,128)(2,1)} %param.10) | copy-start | bytes 49156
  6.5 84.2 %all-gather.2.cloned.1.call-start = ((), (), s32[]{:S(2)}) async-start(), calls=%async_computation.1 | async-start | bytes 6963200 | tf_op jit(solution)/shard_map/all_gather | solution.py:58
  24.2 28.5 %copy-start.1 = (bf16[16,128,128]{2,1,0:T(8,128)(2,1)S(1)}, bf16[16,128,128]{2,1,0:T(8,128)(2,1)}, u32[]{:S(2)}) copy-start(bf16[16,128,128]{2,1,0:T(8,128)(2,1)} %param.11) | copy-start | bytes 1572868
  46.0 6.7 %copy-start.2 = (bf16[16,128,128]{2,1,0:T(8,128)(2,1)S(1)}, bf16[16,128,128]{2,1,0:T(8,128)(2,1)}, u32[]{:S(2)}) copy-start(bf16[16,128,128]{2,1,0:T(8,128)(2,1)} %param.12) | copy-start | bytes 1572868
  48.4 5.2 %collective-permute-start = (bf16[64,7,128]{2,1,0:T(8,128)(2,1)S(1)}, bf16[64,7,128]{2,1,0:T(8,128)(2,1)S(1)}, u32[]{:S(2)}, u32[]{:S(2)}) collective-permute-start(bf16[64,7,128]{2,1,0:T(8,128)(2,1)S(1)} %pad_maximum_fusion.1), channel_id=1, source_target_pairs={{0,8},{8,0},{1,9},{9,1},{2,10},{10,2},{3,11},{11,3},{4,12},{12,4},... | collective-permute-start | bytes 344072 | tf_op jit(solution)/shard_map/ppermute | solution.py:16
  54.7 2.2 %copy-start = (f32[128,5,1024]{2,0,1:T(8,128)}, f32[128,5,1024]{2,0,1:T(8,128)S(1)}, u32[]{:S(2)}) copy-start(f32[128,5,1024]{2,0,1:T(8,128)S(1)} %get-tuple-element.38) | copy-start | bytes 7864324
  61.1 3.4 %collective-permute-start.1 = (bf16[64,1,5,130]{3,0,2,1:T(8,128)(2,1)S(1)}, bf16[64,1,5,130]{3,0,2,1:T(8,128)(2,1)S(1)}, u32[]{:S(2)}, u32[]{:S(2)}) collective-permute-start(bf16[64,1,5,130]{3,0,2,1:T(8,128)(2,1)S(1)} %pad_maximum_fusion), channel_id=1, source_target_pairs={{0,8},{8,0},{1,9},{9,1},{2,10},{10,2},{3,11},{11,3},{4,12},{12,4},... | collective-permute-start | bytes 249608 | tf_op jit(solution)/shard_map/ppermute | solution.py:16
Sparse Core Ops, SparseCore 0:
  46.2 43.5 all-gather.1
where the time goes:
time: 135 us
  blocking collectives  90.9 us (67%)
  between operations  15.1 us (11%)
  matrix products  9.93 us (7%)
  local copies, waits for them, and re-layouts  9.09 us (7%)
  other arithmetic  4.56 us (3%)
  starting transfers between devices  4.38 us (3%)
    all_gather x1, blocking collectives, shards(): gathered = lax.all_gather(projected, 'tp', axis=2, tiled=True)  27.6 us
    all_gather x1, blocking collectives, shards(): full_rows = lax.all_gather(attention[:, None], 'tp', axis=1, tiled=True)  25.7 us
    all_gather x1, blocking collectives, output_rows(): near = lax.all_gather(mine, 'z', axis=0, tiled=True)  21 us
    all_to_all x1, blocking collectives, output_rows(): lax.all_to_all(w_out.reshape(parts, share, width), 'tp', 0, 0, tiled=True)  16.7 us
    dot_general x1, matrix products, shards(): lax.dot_general(full_rows, weights_mine, (((1, 2), (1, 2)), ((), ())), pr...  4.94 us
    ppermute x2, starting transfers between devices, from_partner(): lax.ppermute(value, axis, [(i, i ^ 1 << distance) for i in range(lax.axis...  4.35 us
    dot_general x3, matrix products, absorb(): jnp.einsum('cgqk,kcd->qcgd', weights.astype(jnp.bfloat16), block_values,...  3.52 us
    reshape x1, local copies, waits for them, and re-layouts, shards(): return gathered.reshape(own_rows, -1)  2.92 us
  transfers between devices with their start and end apart: 3, of which 1 were waited for; matrix products, arithmetic and copies ran while one was open for 9% of the time, Pallas kernels for 0%

commit v1 on v0

--- a/solution.py
+++ b/solution.py
@@ -177,7 +177,12 @@
     projected = projected.reshape(own_rows, -1, depth, share)
     projected = jnp.transpose(projected, (0, 2, 1, 3)).reshape(own_rows, -1, share)
     projected = projected.astype(jnp.bfloat16)
-    gathered = lax.all_gather(projected, "tp", axis=2, tiled=True)
+    ring = [projected]
+    for hop in range(7):
+        ring.append(lax.ppermute(ring[-1], "tp", [(dev, (dev + 1) % 8) for dev in range(8)]))
+    gathered = jnp.roll(
+        jnp.concatenate(ring[::-1], axis=2), (lax.axis_index("tp") + 1) * ring[0].shape[2], axis=2
+    )
     return gathered.reshape(own_rows, -1)
 
 

time: 135 us -> 171 us (1.27)
  waiting for transfers between devices: 1.02 us -> 47.7 us
  blocking collectives: 90.9 us -> 63.3 us
  starting transfers between devices: 4.38 us -> 18.8 us
    ppermute x0 -> x7, waiting for transfers between devices: none -> 46.6 us  [shards(): lax.ppermute(ring[-1], 'tp', [(dev, (dev + 1) % 8) for dev in range(8)])]
    all_gather x1 -> x0, blocking collectives: 27.6 us -> none  [shards(): gathered = lax.all_gather(projected, 'tp', axis=2, tiled=True)]
    ppermute x0 -> x7, starting transfers between devices: none -> 14.4 us  [shards(): lax.ppermute(ring[-1], 'tp', [(dev, (dev + 1) % 8) for dev in range(8)])]
    dynamic_slice x0 -> x2, local copies, waits for them, and re-layouts: none -> 2.53 us  [shards(): jnp.roll(jnp.concatenate(ring[::-1], axis=2), (lax.axis_index('tp') + 1)...]
  transfers between devices with their start and end apart: 3 -> 10, of which waited for: 1 -> 8; matrix products, arithmetic and copies ran while one was open for 9% -> 7% of each run, Pallas kernels for 0% -> 0%
where the time goes in v1:
time: 171 us; the launch traced here: 170 us
  blocking collectives  63.3 us (37%)
  waiting for transfers between devices  47.7 us (28%)
  starting transfers between devices  18.8 us (11%)
  between operations  15.3 us (9%)
  local copies, waits for them, and re-layouts  10.4 us (6%)
  matrix products  9.93 us (6%)
  other arithmetic  4.56 us (3%)
    ppermute x7, waiting for transfers between devices, shards(): lax.ppermute(ring[-1], 'tp', [(dev, (dev + 1) % 8) for dev in range(8)])  46.6 us
    all_gather x1, blocking collectives, shards(): full_rows = lax.all_gather(attention[:, None], 'tp', axis=1, tiled=True)  25.7 us
    all_gather x1, blocking collectives, output_rows(): near = lax.all_gather(mine, 'z', axis=0, tiled=True)  21 us
    all_to_all x1, blocking collectives, output_rows(): lax.all_to_all(w_out.reshape(parts, share, width), 'tp', 0, 0, tiled=True)  16.7 us
    ppermute x7, starting transfers between devices, shards(): lax.ppermute(ring[-1], 'tp', [(dev, (dev + 1) % 8) for dev in range(8)])  14.4 us
    dot_general x1, matrix products, shards(): lax.dot_general(full_rows, weights_mine, (((1, 2), (1, 2)), ((), ())), pr...  4.94 us
    ppermute x2, starting transfers between devices, from_partner(): lax.ppermute(value, axis, [(i, i ^ 1 << distance) for i in range(lax.axis...  4.35 us
    dot_general x3, matrix products, absorb(): jnp.einsum('cgqk,kcd->qcgd', weights.astype(jnp.bfloat16), block_values,...  3.52 us
  transfers between devices with their start and end apart: 10, of which 8 were waited for; matrix products, arithmetic and copies ran while one was open for 7% of the time, Pallas kernels for 0%

profile of v1, /device:TPU:6, one launch (start us, length us, event | category | flops | bytes accessed | tf_op | source)
XLA Modules:
  0.0 170.0 jit_solution(14512585018866489349)
XLA Ops:
  6.6 1.0 reshape.452
  7.6 16.7 %all_to_all.5 = bf16[8,10,640]{2,1,0:T(8,128)(2,1)S(1)} all-to-all(bf16[8,10,640]{2,1,0:T(8,128)(2,1)S(1)} %reshape.452), channel_id=1, replica_groups=mesh['z'=4,'x'=8,'core'=2,'tp'=8] {'tp'}, dimensions={0} | all-to-all | bytes 204800 | tf_op jit(solution)/shard_map/all_to_all | solution.py:55
  24.3 21.0 %all_gather.10 = bf16[40,8,640]{2,1,0:T(8,128)(2,1)S(1)} all-gather(bf16[10,8,640]{2,1,0:T(8,128)(2,1)S(1)} %copy.91), channel_id=1, replica_groups=mesh['z'=4,'x'=8,'core'=2,'tp'=8] {'z'}, dimensions={0}, use_global_device_ids=true | all-gather | bytes 512000 | tf_op jit(solution)/shard_map/all_gather | solution.py:57
  45.3 0.8 copy.92
  46.2 0.6 dynamic_slice.28
  47.5 0.2 multiply_cosine_fusion
  48.0 0.1 slice_negate_fusion
  48.2 0.1 fusion.41
  48.3 0.1 pad_maximum_fusion.1
  48.4 1.9 %collective-permute-start = (bf16[64,7,128]{2,1,0:T(8,128)(2,1)S(1)}, bf16[64,7,128]{2,1,0:T(8,128)(2,1)S(1)}, u32[]{:S(2)}, u32[]{:S(2)}) collective-permute-start(bf16[64,7,128]{2,1,0:T(8,128)(2,1)S(1)} %pad_maximum_fusion.1), channel_id=1, source_target_pairs={{0,8},{8,0},{1,9},{9,1},{2,10},{10,2},{3,11},{11,3},{4,12},{12,4},... | collective-permute-start | bytes 344072 | tf_op jit(solution)/shard_map/ppermute | solution.py:16
  51.1 0.7 fusion.97
  51.8 0.1 fusion.77
  51.9 0.1 select_reduce_fusion
  52.0 0.7 fusion.79
  52.8 0.8 fusion.110
  53.7 0.1 maximum_select_fusion
  53.9 0.2 fusion.113
  54.1 0.6 fusion.2
  54.7 0.6 fusion.3
  55.4 1.5 fusion.4
  57.0 0.1 copy.86
  57.3 0.1 copy.87
  57.4 0.3 fusion.35
  57.7 2.5 %fusion.31 = f32[128,1,5,128]{3,0,2,1:T(8,128)S(1)} fusion(f32[128,1,5,128]{3,0,2,1:T(8,128)S(1)} %fusion.35, bf16[1024,128,1]{1,0,2:T(8,128)(2,1)} %bitcast.313, f32[128,5,1024]{2,0,1:T(8,128)} %copy-done, f32[5,128]{1,0:T(8,128)S(1)} %get-tuple-element.10, pred[1024]{0:T(1024)(128)(4,1)S(1)} %get-tuple-element.8, f32[128,5]{0,1:T(8,128)S(1)} %get-tuple-element.24), kind=kOutput, calls=%fused_computation.27 | convolution fusion | flops 171212800 | bytes 3545088 | tf_op jit(solution)/shard_map/cgqk,kcd->qcgd/dot_general | solution.py:41
  60.2 0.7 fusion.28
  61.1 2.4 %collective-permute-start.1 = (bf16[64,1,5,130]{3,0,2,1:T(8,128)(2,1)S(1)}, bf16[64,1,5,130]{3,0,2,1:T(8,128)(2,1)S(1)}, u32[]{:S(2)}, u32[]{:S(2)}) collective-permute-start(bf16[64,1,5,130]{3,0,2,1:T(8,128)(2,1)S(1)} %pad_maximum_fusion), channel_id=1, source_target_pairs={{0,8},{8,0},{1,9},{9,1},{2,10},{10,2},{3,11},{11,3},{4,12},{12,4},... | collective-permute-start | bytes 249608 | tf_op jit(solution)/shard_map/ppermute | solution.py:16
  63.5 1.0 collective-permute-done.1
  64.5 0.2 slice_reduce_fusion.1
  64.8 0.2 copy_bitcast_fusion
  65.1 25.7 %all_gather.9 = bf16[64,8,640]{2,0,1:T(8,128)(2,1)S(1)} all-gather(bf16[64,1,640]{2,0,1:T(8,128)(2,1)S(1)} %copy_bitcast_fusion), channel_id=1, replica_groups=mesh['z'=4,'x'=8,'core'=2,'tp'=8] {'tp'}, dimensions={1}, use_global_device_ids=true | all-gather | bytes 737280 | tf_op jit(solution)/shard_map/all_gather | solution.py:172
  90.7 4.9 %fusion.37 = bf16[64,640]{1,0:T(8,128)(2,1)S(1)} fusion(bf16[64,8,640]{2,0,1:T(8,128)(2,1)S(1)} %all_gather.9, bf16[640,8,640]{2,0,1:T(8,128)(2,1)} %all-gather.2.cloned.1.call-done), kind=kOutput, calls=%fused_computation.32 | convolution fusion | flops 419471360 | bytes 7290880 | tf_op jit(solution)/shard_map/dot_general | solution.py:173
  95.7 0.2 copy.93
  96.0 2.5 %collective-permute-start.2 = (bf16[64,64,10]{0,1,2:T(8,128)(2,1)S(1)}, bf16[64,64,10]{0,1,2:T(8,128)(2,1)S(1)}, u32[]{:S(2)}, u32[]{:S(2)}) collective-permute-start(bf16[64,64,10]{0,1,2:T(8,128)(2,1)S(1)} %bitcast.304), channel_id=1, source_target_pairs={{0,1},{1,2},{2,3},{3,4},{4,5},{5,6},{6,7},{7,0},{8,9},{9,10},{10,1... | collective-permute-start | bytes 245768 | tf_op jit(solution)/shard_map/ppermute | solution.py:182
  98.5 6.0 %collective-permute-done.2 = bf16[64,64,10]{0,1,2:T(8,128)(2,1)S(1)} collective-permute-done((bf16[64,64,10]{0,1,2:T(8,128)(2,1)S(1)}, bf16[64,64,10]{0,1,2:T(8,128)(2,1)S(1)}, u32[]{:S(2)}, u32[]{:S(2)}) %collective-permute-start.2) | collective-permute-done | bytes 81952 | tf_op jit(solution)/shard_map/ppermute | solution.py:182
  104.6 2.2 %collective-permute-start.3 = (bf16[64,64,10]{0,1,2:T(8,128)(2,1)S(1)}, bf16[64,64,10]{0,1,2:T(8,128)(2,1)S(1)}, u32[]{:S(2)}, u32[]{:S(2)}) collective-permute-start(bf16[64,64,10]{0,1,2:T(8,128)(2,1)S(1)} %collective-permute-done.2), channel_id=1, source_target_pairs={{0,1},{1,2},{2,3},{3,4},{4,5},{5,6},{6,7},{7,0},{8,9},{9,10},{10,1... | collective-permute-start | bytes 245768 | tf_op jit(solution)/shard_map/ppermute | solution.py:182
  106.8 6.2 %collective-permute-done.3 = bf16[64,64,10]{0,1,2:T(8,128)(2,1)S(1)} collective-permute-done((bf16[64,64,10]{0,1,2:T(8,128)(2,1)S(1)}, bf16[64,64,10]{0,1,2:T(8,128)(2,1)S(1)}, u32[]{:S(2)}, u32[]{:S(2)}) %collective-permute-start.3) | collective-permute-done | bytes 81952 | tf_op jit(solution)/shard_map/ppermute | solution.py:182
  113.0 1.9 %collective-permute-start.4 = (bf16[64,64,10]{0,1,2:T(8,128)(2,1)S(1)}, bf16[64,64,10]{0,1,2:T(8,128)(2,1)S(1)}, u32[]{:S(2)}, u32[]{:S(2)}) collective-permute-start(bf16[64,64,10]{0,1,2:T(8,128)(2,1)S(1)} %collective-permute-done.3), channel_id=1, source_target_pairs={{0,1},{1,2},{2,3},{3,4},{4,5},{5,6},{6,7},{7,0},{8,9},{9,10},{10,1... | collective-permute-start | bytes 245768 | tf_op jit(solution)/shard_map/ppermute | solution.py:182
  114.9 6.5 %collective-permute-done.4 = bf16[64,64,10]{0,1,2:T(8,128)(2,1)S(1)} collective-permute-done((bf16[64,64,10]{0,1,2:T(8,128)(2,1)S(1)}, bf16[64,64,10]{0,1,2:T(8,128)(2,1)S(1)}, u32[]{:S(2)}, u32[]{:S(2)}) %collective-permute-start.4) | collective-permute-done | bytes 81952 | tf_op jit(solution)/shard_map/ppermute | solution.py:182
  121.4 1.9 %collective-permute-start.5 = (bf16[64,64,10]{0,1,2:T(8,128)(2,1)S(1)}, bf16[64,64,10]{0,1,2:T(8,128)(2,1)S(1)}, u32[]{:S(2)}, u32[]{:S(2)}) collective-permute-start(bf16[64,64,10]{0,1,2:T(8,128)(2,1)S(1)} %collective-permute-done.4), channel_id=1, source_target_pairs={{0,1},{1,2},{2,3},{3,4},{4,5},{5,6},{6,7},{7,0},{8,9},{9,10},{10,1... | collective-permute-start | bytes 245768 | tf_op jit(solution)/shard_map/ppermute | solution.py:182
  123.3 6.5 %collective-permute-done.5 = bf16[64,64,10]{0,1,2:T(8,128)(2,1)S(1)} collective-permute-done((bf16[64,64,10]{0,1,2:T(8,128)(2,1)S(1)}, bf16[64,64,10]{0,1,2:T(8,128)(2,1)S(1)}, u32[]{:S(2)}, u32[]{:S(2)}) %collective-permute-start.5) | collective-permute-done | bytes 81952 | tf_op jit(solution)/shard_map/ppermute | solution.py:182
  129.8 1.9 %collective-permute-start.6 = (bf16[64,64,10]{0,1,2:T(8,128)(2,1)S(1)}, bf16[64,64,10]{0,1,2:T(8,128)(2,1)S(1)}, u32[]{:S(2)}, u32[]{:S(2)}) collective-permute-start(bf16[64,64,10]{0,1,2:T(8,128)(2,1)S(1)} %collective-permute-done.5), channel_id=1, source_target_pairs={{0,1},{1,2},{2,3},{3,4},{4,5},{5,6},{6,7},{7,0},{8,9},{9,10},{10,1... | collective-permute-start | bytes 245768 | tf_op jit(solution)/shard_map/ppermute | solution.py:182
  131.7 7.0 %collective-permute-done.6 = bf16[64,64,10]{0,1,2:T(8,128)(2,1)S(1)} collective-permute-done((bf16[64,64,10]{0,1,2:T(8,128)(2,1)S(1)}, bf16[64,64,10]{0,1,2:T(8,128)(2,1)S(1)}, u32[]{:S(2)}, u32[]{:S(2)}) %collective-permute-start.6) | collective-permute-done | bytes 81952 | tf_op jit(solution)/shard_map/ppermute | solution.py:182
  138.7 1.9 %collective-permute-start.7 = (bf16[64,64,10]{0,1,2:T(8,128)(2,1)S(1)}, bf16[64,64,10]{0,1,2:T(8,128)(2,1)S(1)}, u32[]{:S(2)}, u32[]{:S(2)}) collective-permute-start(bf16[64,64,10]{0,1,2:T(8,128)(2,1)S(1)} %collective-permute-done.6), channel_id=1, source_target_pairs={{0,1},{1,2},{2,3},{3,4},{4,5},{5,6},{6,7},{7,0},{8,9},{9,10},{10,1... | collective-permute-start | bytes 245768 | tf_op jit(solution)/shard_map/ppermute | solution.py:182
  140.6 8.1 %collective-permute-done.7 = bf16[64,64,10]{0,1,2:T(8,128)(2,1)S(1)} collective-permute-done((bf16[64,64,10]{0,1,2:T(8,128)(2,1)S(1)}, bf16[64,64,10]{0,1,2:T(8,128)(2,1)S(1)}, u32[]{:S(2)}, u32[]{:S(2)}) %collective-permute-start.7) | collective-permute-done | bytes 81952 | tf_op jit(solution)/shard_map/ppermute | solution.py:182
  148.7 2.1 %collective-permute-start.8 = (bf16[64,64,10]{0,1,2:T(8,128)(2,1)S(1)}, bf16[64,64,10]{0,1,2:T(8,128)(2,1)S(1)}, u32[]{:S(2)}, u32[]{:S(2)}) collective-permute-start(bf16[64,64,10]{0,1,2:T(8,128)(2,1)S(1)} %collective-permute-done.7), channel_id=1, source_target_pairs={{0,1},{1,2},{2,3},{3,4},{4,5},{5,6},{6,7},{7,0},{8,9},{9,10},{10,1... | collective-permute-start | bytes 245768 | tf_op jit(solution)/shard_map/ppermute | solution.py:182
  150.9 6.3 %collective-permute-done.8 = bf16[64,64,10]{0,1,2:T(8,128)(2,1)S(1)} collective-permute-done((bf16[64,64,10]{0,1,2:T(8,128)(2,1)S(1)}, bf16[64,64,10]{0,1,2:T(8,128)(2,1)S(1)}, u32[]{:S(2)}, u32[]{:S(2)}) %collective-permute-start.8) | collective-permute-done | bytes 81952 | tf_op jit(solution)/shard_map/ppermute | solution.py:182
  157.7 2.4 %copy.95 = bf16[64,64,80]{2,1,0:T(8,128)(2,1)S(1)} copy(bf16[64,64,80]{0,1,2:T(8,128)(2,1)S(1)} %constant_dynamic-slice_fusion) | data formatting | bytes 1310720 | tf_op jit(solution)/shard_map/jit(_roll_dynamic)/dynamic_slice | solution.py:183
  160.2 2.9 %reshape.453 = bf16[64,5120]{1,0:T(8,128)(2,1)} reshape(bf16[64,64,80]{2,1,0:T(8,128)(2,1)S(1)} %copy.95) | data formatting | bytes 1310720 | tf_op jit(solution)/shard_map/reshape | solution.py:186
  (64 shorter events, 1.8 us)
Async XLA Ops:
  6.5 39.6 %copy-start.3 = (bf16[64,640]{1,0:T(8,128)(2,1)S(1)}, bf16[64,640]{1,0:T(8,128)(2,1)}, u32[]{:S(2)}) copy-start(bf16[64,640]{1,0:T(8,128)(2,1)} %param.8) | copy-start | bytes 245764
  6.5 39.7 %copy-start.6 = (s32[32]{0:T(128)S(1)}, s32[32]{0:T(128)}, u32[]{:S(2)}) copy-start(s32[32]{0:T(128)} %param.13) | copy-start | bytes 388
  6.5 41.0 %copy-start.4 = (bf16[64,128]{1,0:T(8,128)(2,1)S(1)}, bf16[64,128]{1,0:T(8,128)(2,1)}, u32[]{:S(2)}) copy-start(bf16[64,128]{1,0:T(8,128)(2,1)} %param.9) | copy-start | bytes 49156
  6.5 41.4 %copy-start.5 = (bf16[64,128]{1,0:T(8,128)(2,1)S(1)}, bf16[64,128]{1,0:T(8,128)(2,1)}, u32[]{:S(2)}) copy-start(bf16[64,128]{1,0:T(8,128)(2,1)} %param.10) | copy-start | bytes 49156
  6.5 84.2 %all-gather.2.cloned.1.call-start = ((), (), s32[]{:S(2)}) async-start(), calls=%async_computation.1 | async-start | bytes 6963200 | tf_op jit(solution)/shard_map/all_gather | solution.py:58
  24.2 28.5 %copy-start.1 = (bf16[16,128,128]{2,1,0:T(8,128)(2,1)S(1)}, bf16[16,128,128]{2,1,0:T(8,128)(2,1)}, u32[]{:S(2)}) copy-start(bf16[16,128,128]{2,1,0:T(8,128)(2,1)} %param.11) | copy-start | bytes 1572868
  46.0 6.7 %copy-start.2 = (bf16[16,128,128]{2,1,0:T(8,128)(2,1)S(1)}, bf16[16,128,128]{2,1,0:T(8,128)(2,1)}, u32[]{:S(2)}) copy-start(bf16[16,128,128]{2,1,0:T(8,128)(2,1)} %param.12) | copy-start | bytes 1572868
  48.4 5.2 %collective-permute-start = (bf16[64,7,128]{2,1,0:T(8,128)(2,1)S(1)}, bf16[64,7,128]{2,1,0:T(8,128)(2,1)S(1)}, u32[]{:S(2)}, u32[]{:S(2)}) collective-permute-start(bf16[64,7,128]{2,1,0:T(8,128)(2,1)S(1)} %pad_maximum_fusion.1), channel_id=1, source_target_pairs={{0,8},{8,0},{1,9},{9,1},{2,10},{10,2},{3,11},{11,3},{4,12},{12,4},... | collective-permute-start | bytes 344072 | tf_op jit(solution)/shard_map/ppermute | solution.py:16
  54.7 2.2 %copy-start = (f32[128,5,1024]{2,0,1:T(8,128)}, f32[128,5,1024]{2,0,1:T(8,128)S(1)}, u32[]{:S(2)}) copy-start(f32[128,5,1024]{2,0,1:T(8,128)S(1)} %get-tuple-element.38) | copy-start | bytes 7864324
  61.1 3.4 %collective-permute-start.1 = (bf16[64,1,5,130]{3,0,2,1:T(8,128)(2,1)S(1)}, bf16[64,1,5,130]{3,0,2,1:T(8,128)(2,1)S(1)}, u32[]{:S(2)}, u32[]{:S(2)}) collective-permute-start(bf16[64,1,5,130]{3,0,2,1:T(8,128)(2,1)S(1)} %pad_maximum_fusion), channel_id=1, source_target_pairs={{0,8},{8,0},{1,9},{9,1},{2,10},{10,2},{3,11},{11,3},{4,12},{12,4},... | collective-permute-start | bytes 249608 | tf_op jit(solution)/shard_map/ppermute | solution.py:16
  96.0 8.5 %collective-permute-start.2 = (bf16[64,64,10]{0,1,2:T(8,128)(2,1)S(1)}, bf16[64,64,10]{0,1,2:T(8,128)(2,1)S(1)}, u32[]{:S(2)}, u32[]{:S(2)}) collective-permute-start(bf16[64,64,10]{0,1,2:T(8,128)(2,1)S(1)} %bitcast.304), channel_id=1, source_target_pairs={{0,1},{1,2},{2,3},{3,4},{4,5},{5,6},{6,7},{7,0},{8,9},{9,10},{10,1... | collective-permute-start | bytes 245768 | tf_op jit(solution)/shard_map/ppermute | solution.py:182
  104.6 8.4 %collective-permute-start.3 = (bf16[64,64,10]{0,1,2:T(8,128)(2,1)S(1)}, bf16[64,64,10]{0,1,2:T(8,128)(2,1)S(1)}, u32[]{:S(2)}, u32[]{:S(2)}) collective-permute-start(bf16[64,64,10]{0,1,2:T(8,128)(2,1)S(1)} %collective-permute-done.2), channel_id=1, source_target_pairs={{0,1},{1,2},{2,3},{3,4},{4,5},{5,6},{6,7},{7,0},{8,9},{9,10},{10,1... | collective-permute-start | bytes 245768 | tf_op jit(solution)/shard_map/ppermute | solution.py:182
  113.0 8.4 %collective-permute-start.4 = (bf16[64,64,10]{0,1,2:T(8,128)(2,1)S(1)}, bf16[64,64,10]{0,1,2:T(8,128)(2,1)S(1)}, u32[]{:S(2)}, u32[]{:S(2)}) collective-permute-start(bf16[64,64,10]{0,1,2:T(8,128)(2,1)S(1)} %collective-permute-done.3), channel_id=1, source_target_pairs={{0,1},{1,2},{2,3},{3,4},{4,5},{5,6},{6,7},{7,0},{8,9},{9,10},{10,1... | collective-permute-start | bytes 245768 | tf_op jit(solution)/shard_map/ppermute | solution.py:182
  121.4 8.4 %collective-permute-start.5 = (bf16[64,64,10]{0,1,2:T(8,128)(2,1)S(1)}, bf16[64,64,10]{0,1,2:T(8,128)(2,1)S(1)}, u32[]{:S(2)}, u32[]{:S(2)}) collective-permute-start(bf16[64,64,10]{0,1,2:T(8,128)(2,1)S(1)} %collective-permute-done.4), channel_id=1, source_target_pairs={{0,1},{1,2},{2,3},{3,4},{4,5},{5,6},{6,7},{7,0},{8,9},{9,10},{10,1... | collective-permute-start | bytes 245768 | tf_op jit(solution)/shard_map/ppermute | solution.py:182
  129.8 8.9 %collective-permute-start.6 = (bf16[64,64,10]{0,1,2:T(8,128)(2,1)S(1)}, bf16[64,64,10]{0,1,2:T(8,128)(2,1)S(1)}, u32[]{:S(2)}, u32[]{:S(2)}) collective-permute-start(bf16[64,64,10]{0,1,2:T(8,128)(2,1)S(1)} %collective-permute-done.5), channel_id=1, source_target_pairs={{0,1},{1,2},{2,3},{3,4},{4,5},{5,6},{6,7},{7,0},{8,9},{9,10},{10,1... | collective-permute-start | bytes 245768 | tf_op jit(solution)/shard_map/ppermute | solution.py:182
  138.7 10.0 %collective-permute-start.7 = (bf16[64,64,10]{0,1,2:T(8,128)(2,1)S(1)}, bf16[64,64,10]{0,1,2:T(8,128)(2,1)S(1)}, u32[]{:S(2)}, u32[]{:S(2)}) collective-permute-start(bf16[64,64,10]{0,1,2:T(8,128)(2,1)S(1)} %collective-permute-done.6), channel_id=1, source_target_pairs={{0,1},{1,2},{2,3},{3,4},{4,5},{5,6},{6,7},{7,0},{8,9},{9,10},{10,1... | collective-permute-start | bytes 245768 | tf_op jit(solution)/shard_map/ppermute | solution.py:182
  148.7 8.4 %collective-permute-start.8 = (bf16[64,64,10]{0,1,2:T(8,128)(2,1)S(1)}, bf16[64,64,10]{0,1,2:T(8,128)(2,1)S(1)}, u32[]{:S(2)}, u32[]{:S(2)}) collective-permute-start(bf16[64,64,10]{0,1,2:T(8,128)(2,1)S(1)} %collective-permute-done.7), channel_id=1, source_target_pairs={{0,1},{1,2},{2,3},{3,4},{4,5},{5,6},{6,7},{7,0},{8,9},{9,10},{10,1... | collective-permute-start | bytes 245768 | tf_op jit(solution)/shard_map/ppermute | solution.py:182
Sparse Core Ops, SparseCore 0:
  46.2 43.5 all-gather.1
